TPU v7x, 256 devices: a whole 4x4x8 slice. The times are simulated.
256 devices in a mesh: tile: 32 (over x, z), atom: 8 (over y, core).
Axes of the slice: x: 4, y: 4, z: 8, core: 2. Of those that a mesh axis runs over, the one named last changes fastest.
Arguments:
- images: float32 [1024, 1024], P(('tile', 'atom')), may hold values from -6 to 6
- active: int32 [1024, 2], P(('tile', 'atom')), may hold values from 0 to 7, all different within a row; in each aligned block of 4 rows (0 to 3, 4 to 7, ...) at most 2 rows name the same one
- dictionary: float32 [8, 32, 1024], P('atom', 'tile'), may hold values from -6 to 6
Outputs:
- reconstruction: float32 [1024, 1024], P(('tile', 'atom'))
- new_dictionary: float32 [8, 32, 1024], P('atom', 'tile')
Inputs may be any that keep to these rules, and one draw needn't show every extreme that they name: `active`: each tile names 2 different atom blocks. Among the 4 tiles of one device no block is named by more than 2 tiles, and on some devices one block is named by exactly 2. Every block is named by some tile.
All inputs are finite; a program needn't handle non-finite values.
Results may differ from a plain program's by a relative error of at most 0.0001.
Values sent between devices are 32-bit elements; how exact they have to be, the bound alone decides.
No kernel may reach another device: no remote copies, remote signals or barrier semaphores. Data moves between devices by JAX's collectives and lax.ppermute only.
A program may use at most 128 MiB of HBM per device.

v0:
```python
import math
import jax
import jax.numpy as jnp
from jax import lax
from jax.sharding import PartitionSpec as P

SIDE = 32
BLK = 32
NBLK = 8
ACT = 2
MOST = 2
ITERS = 2
shrink_scale = 0.5
step_ratio = 0.5
epsilon = 1e-06
highest = lax.Precision.HIGHEST


def momentum_weights(count):
    weights = []
    current = 1.0
    for sweep in range(count):
        following = (1.0 + math.sqrt(1.0 + 4.0 * current * current)) / 2.0
        weights.append((current - 1.0) / following)
        current = following
    return weights


def unit_rows(values):
    return values / jnp.sqrt(jnp.mean(values * values, axis=-1, keepdims=True) + epsilon)


def fourier_table(length):
    position = jnp.arange(length, dtype=jnp.int32)
    phase = position[:, None] * position[None, :] % length
    angle = phase.astype(jnp.float32) * (2.0 * math.pi / length)
    cosine = jnp.cos(angle)
    sine = jnp.sin(angle)
    forward_right = jnp.stack([cosine, -sine], axis=1)
    forward_left = jnp.stack(
        [jnp.stack([cosine, sine], axis=1), jnp.stack([-sine, cosine], axis=1)], axis=0
    )
    inverse_right = jnp.stack(
        [jnp.stack([cosine, sine], axis=1), jnp.stack([-sine, cosine], axis=1)], axis=0
    )
    inverse_left = jnp.stack([cosine, -sine], axis=0)
    return (forward_right, forward_left, inverse_right, inverse_left)


def forward(values, table):
    forward_right, forward_left = (table[0], table[1])
    length = forward_right.shape[0]
    field = values.reshape(values.shape[:-1] + (length, length))
    across = jnp.einsum(
        "...uw,wdq->...udq",
        field,
        forward_right,
        precision=highest,
        preferred_element_type=jnp.float32,
    )
    result = jnp.einsum(
        "cpdu,...udq->...cpq",
        forward_left,
        across,
        precision=highest,
        preferred_element_type=jnp.float32,
    )
    return result.reshape(values.shape[:-1] + (2 * length * length,))


def inverse(spectra, table):
    inverse_right, inverse_left = (table[2], table[3])
    length = inverse_left.shape[1]
    shaped = spectra.reshape(spectra.shape[:-1] + (2, length, length))
    across = jnp.einsum(
        "...cpq,cqew->...pew",
        shaped,
        inverse_right,
        precision=highest,
        preferred_element_type=jnp.float32,
    )
    result = jnp.einsum(
        "lmq,...qlg->...mg",
        inverse_left,
        across,
        precision=highest,
        preferred_element_type=jnp.float32,
    )
    return result.reshape(spectra.shape[:-1] + (length * length,)) / (length * length)


def split_parts(packed):
    middle = packed.shape[-1] // 2
    return (packed[..., :middle], packed[..., middle:])


def times_conj(first, second):
    first_real, first_imag = split_parts(first)
    second_real, second_imag = split_parts(second)
    real_part = first_real * second_real + first_imag * second_imag
    imag_part = first_real * second_imag - first_imag * second_real
    return jnp.concatenate([real_part, imag_part], axis=-1)


def product_sum(atom_spec, code_spec):
    atom_real, atom_imag = split_parts(atom_spec)
    code_real, code_imag = split_parts(code_spec)
    real_sum = jnp.sum(atom_real * code_real - atom_imag * code_imag, axis=(1, 2))
    imag_sum = jnp.sum(atom_real * code_imag + atom_imag * code_real, axis=(1, 2))
    return jnp.concatenate([real_sum, imag_sum], axis=-1)


def on_device(images, active, dictionary):
    tiles_here = images.shape[0]
    pixels = images.shape[1]
    rows_owned = dictionary.shape[1]
    table = fourier_table(SIDE)
    image_spec = forward(images, table)
    atoms = unit_rows(dictionary)
    slot_count = tiles_here * ACT
    flat_ids = active.reshape(slot_count)
    block_range = jnp.arange(NBLK, dtype=jnp.int32)
    slot_index = jnp.arange(slot_count, dtype=jnp.int32)
    earlier = slot_index[None, :] < slot_index[:, None]
    same_block = flat_ids[:, None] == flat_ids[None, :]
    rank = jnp.sum((earlier & same_block).astype(jnp.int32), axis=1)
    slot_range = jnp.arange(MOST, dtype=jnp.int32)
    placing = (block_range[:, None, None] == flat_ids[None, None, :]) & (
        slot_range[None, :, None] == rank[None, None, :]
    )
    placing = placing.astype(jnp.float32).reshape(NBLK * MOST, slot_count)
    codes = jnp.zeros((tiles_here, ACT, BLK, pixels), jnp.float32)
    code_spec = jnp.zeros((tiles_here, ACT, BLK, 2 * pixels), jnp.float32)
    weights = momentum_weights(ITERS)
    own_spec = forward(atoms, table)
    every = lax.all_gather(own_spec, ("tile", "atom"), axis=0, tiled=True)
    tile_groups = lax.axis_size("tile")
    every = every.reshape(tile_groups, NBLK, rows_owned, 2 * pixels)
    chosen = jnp.take(every, flat_ids, axis=1)
    chosen = jnp.transpose(chosen, (1, 0, 2, 3)).reshape(tiles_here, ACT, BLK, 2 * pixels)
    chosen_real, chosen_imag = split_parts(chosen)
    power = chosen_real * chosen_real + chosen_imag * chosen_imag
    bound = jnp.max(jnp.sum(power, axis=(1, 2)), axis=1) + epsilon
    rate = (1.0 / bound)[:, None, None, None]
    limit = rate * (shrink_scale * SIDE)
    prior = codes
    prior_spec = code_spec
    guess = codes
    guess_spec = code_spec
    for sweep in range(ITERS):
        residual_spec = product_sum(chosen, guess_spec) - image_spec
        gradient = inverse(times_conj(chosen, residual_spec[:, None, None, :]), table)
        moved = guess - rate * gradient
        fresh = moved - jnp.clip(moved, -limit, limit)
        fresh_spec = forward(fresh, table)
        guess = fresh + weights[sweep] * (fresh - prior)
        guess_spec = fresh_spec + weights[sweep] * (fresh_spec - prior_spec)
        prior, prior_spec = (fresh, fresh_spec)
    recon_spec = product_sum(chosen, prior_spec)
    residual_spec = recon_spec - image_spec
    slot_terms = times_conj(prior_spec, residual_spec[:, None, None, :]).reshape(
        slot_count, BLK * 2 * pixels
    )
    outgoing = jnp.dot(placing, slot_terms, precision=highest, preferred_element_type=jnp.float32)
    outgoing = outgoing.reshape(NBLK, MOST, BLK, 2 * pixels)
    arrived = lax.all_to_all(outgoing, "atom", split_axis=0, concat_axis=1, tiled=True)
    owner_sum = jnp.sum(arrived, axis=1)
    total = lax.psum(owner_sum, "tile")
    offset = lax.axis_index("tile") * rows_owned
    mine = lax.dynamic_slice_in_dim(total, offset, rows_owned, 1)
    atom_grad = inverse(mine, table)
    scale = jnp.sqrt(jnp.mean(atom_grad * atom_grad, axis=-1, keepdims=True) + epsilon)
    atoms = unit_rows(atoms - step_ratio * atom_grad / scale)
    recon = inverse(recon_spec, table)
    return (recon, atoms)


def solution(mesh):
    in_specs = (P(("tile", "atom"), None), P(("tile", "atom"), None), P("atom", "tile", None))
    out_specs = (P(("tile", "atom"), None), P("atom", "tile", None))
    return jax.shard_map(
        on_device, mesh=mesh, in_specs=in_specs, out_specs=out_specs, check_vma=False
    )
```

profile of v0, /device:TPU:8, one launch (start us, length us, event | category | flops | bytes accessed | tf_op | source)
XLA Modules:
  0.0 500.6 jit_solution(15187165786976593706)
XLA Ops:
  7.2 0.1 fusion.71
  7.3 0.1 fusion.70
  7.4 1.3 multiply_reduce_fusion.2
  9.4 0.5 broadcast.415
  9.9 1.3 fusion.91
  11.3 0.2 convolution_bitcast_fusion.6
  11.6 0.3 convolution_bitcast_fusion.5
  11.9 0.7 reshape.499
  12.6 0.8 copy.66
  13.4 0.1 reshape.501
  13.5 0.1 reshape.497
  13.6 0.8 reshape.527
  14.4 0.5 convolution_bitcast_fusion.2
  14.9 0.3 convolution_bitcast_fusion.1
  15.2 0.1 copy.72
  15.3 0.1 reshape.504
  15.4 0.1 sine_negate_fusion
  15.5 0.2 convert_reduce_fusion
  15.7 104.0 %all-gather.2.cloned.1.call-done = f32[256,1,2048]{2,1,0:T(1,128)} async-done(((f32[1,1,2048]{2,1,0:T(1,128)}), f32[256,1,2048]{2,1,0:T(1,128)}) %all-gather.2.cloned.1.call-update) | async-done | bytes 2097168 | tf_op jit(solution)/shard_map/all_gather | solution.py:136
  119.8 2.5 copy.160
  122.2 1.2 copy.70
  123.5 2.0 gather_fusion
  125.5 1.9 bitcast_select_fusion
  127.4 0.4 add_reduce_fusion.2
  127.9 0.3 multiply_add_fusion.4
  128.2 1.5 pad_maximum_fusion
  129.7 6.5 %reshape.531 = f32[4,2,32,2,32,32,1]{5,4,3,2,1,0,6:T(8,128)} reshape(f32[4,2,32,2048]{3,2,1,0:T(8,128)} %pad_maximum_fusion) | data formatting | bytes 4194304 | tf_op jit(solution)/shard_map/reshape | solution.py:74
  136.2 23.9 %fusion.6 = f32[4,2,32,32,2,32,1]{3,5,4,6,2,1,0:T(8,128)} fusion(f32[4,2,32,2,32,32,1]{5,4,3,2,1,0,6:T(8,128)} %reshape.531, f32[1,32,2,32]{3,1,2,0:T(8,128)S(1)} %get-tuple-element.28, f32[1,32,2,32]{3,1,2,0:T(8,128)S(1)} %get-tuple-element.27), kind=kOutput, calls=%fused_computation.7 | convolution fusion | flops 402657280 | bytes 4210688 | tf_op jit(solution)/shard_map/...cpq,cqew->...pew/dot_general | solution.py:75
  160.1 0.1 reduce_max.9
  160.2 10.9 %fusion.4 = f32[4,2,32,32,32,1]{4,3,5,2,1,0:T(8,128)S(1)} fusion(f32[4,2,32,32,2,32,1]{3,5,4,6,2,1,0:T(8,128)} %fusion.6, f32[1,32,32]{2,1,0:T(8,128)S(1)} %get-tuple-element.35, f32[1,32,32]{2,1,0:T(8,128)S(1)} %get-tuple-element.36), kind=kOutput, calls=%fused_computation.5 | convolution fusion | flops 201328640 | bytes 3153920 | tf_op jit(solution)/shard_map/lmq,...qlg->...mg/dot_general | solution.py:82
  171.2 7.1 %fusion.15 = f32[4,2,32,32,2,32]{3,5,4,2,1,0:T(8,128)S(1)} fusion(f32[4,2,32,32,32,1]{4,3,5,2,1,0:T(8,128)S(1)} %fusion.4, f32[4]{0:T(128)S(1)} %get-tuple-element.30, f32[4]{0:T(128)S(1)} %get-tuple-element.29, f32[4]{0:T(128)S(1)} %get-tuple-element.11, f32[32,1,32]{2,0,1:T(8,128)S(1)} %get-tuple-element.33, f32[32,1,32]{2,0,1:T(8,128)S(1)} %get-tuple-element.34), kind=kOutput, calls=%fused_computation.17 | convolution fusion | flops 202639360 | bytes 3153968 | tf_op jit(solution)/shard_map/...uw,wdq->...udq/dot_general | solution.py:54
  178.4 8.9 %fusion.23 = f32[4,2,32,2,32,32]{4,5,3,2,1,0:T(8,128)} fusion(f32[4,2,32,32,2,32]{3,5,4,2,1,0:T(8,128)S(1)} %fusion.15, f32[1,32,2,32]{3,1,2,0:T(8,128)S(1)} %get-tuple-element.28, f32[1,32,2,32]{3,1,2,0:T(8,128)S(1)} %get-tuple-element.27), kind=kOutput, calls=%fused_computation.28 | convolution fusion | flops 402657280 | bytes 4210688 | tf_op jit(solution)/shard_map/cpdu,...udq->...cpq/dot_general | solution.py:61
  187.3 8.9 %copy.78 = f32[4,2,32,2,32,32]{5,4,3,2,1,0:T(8,128)} copy(f32[4,2,32,2,32,32]{4,5,3,2,1,0:T(8,128)} %fusion.23) | data formatting | bytes 4194304 | tf_op jit(solution)/shard_map/cpdu,...udq->...cpq/transpose | solution.py:61
  196.2 7.6 %reshape.506 = f32[4,2,32,2048]{3,2,1,0:T(8,128)} reshape(f32[4,2,32,2,32,32]{5,4,3,2,1,0:T(8,128)} %copy.78) | data formatting | bytes 4194304 | tf_op jit(solution)/shard_map/reshape | solution.py:68
  203.9 1.8 multiply_add_fusion.1
  205.6 0.6 subtract_reduce_fusion.1
  206.2 0.3 multiply_add_fusion.3
  206.5 1.5 pad_maximum_fusion.1
  208.1 6.3 %reshape.541 = f32[4,2,32,2,32,32,1]{5,4,3,2,1,0,6:T(8,128)} reshape(f32[4,2,32,2048]{3,2,1,0:T(8,128)} %pad_maximum_fusion.1) | data formatting | bytes 4194304 | tf_op jit(solution)/shard_map/reshape | solution.py:74
  214.3 22.6 %fusion.2 = f32[4,2,32,32,2,32,1]{3,5,4,6,2,1,0:T(8,128)S(1)} fusion(f32[4,2,32,2,32,32,1]{5,4,3,2,1,0,6:T(8,128)} %reshape.541, f32[1,32,2,32]{3,1,2,0:T(8,128)S(1)} %get-tuple-element.28, f32[1,32,2,32]{3,1,2,0:T(8,128)S(1)} %get-tuple-element.27), kind=kOutput, calls=%fused_computation.3 | convolution fusion | flops 402657280 | bytes 4210688 | tf_op jit(solution)/shard_map/...cpq,cqew->...pew/dot_general | solution.py:75
  237.0 6.7 %fusion = f32[4,2,32,32,32,1]{4,3,5,2,1,0:T(8,128)S(1)} fusion(f32[4,2,32,32,2,32,1]{3,5,4,6,2,1,0:T(8,128)S(1)} %fusion.2, f32[1,32,32]{2,1,0:T(8,128)S(1)} %get-tuple-element.35, f32[1,32,32]{2,1,0:T(8,128)S(1)} %get-tuple-element.36), kind=kOutput, calls=%fused_computation.1 | convolution fusion | flops 201328640 | bytes 3153920 | tf_op jit(solution)/shard_map/lmq,...qlg->...mg/dot_general | solution.py:82
  243.6 8.9 %fusion.13 = f32[4,2,32,32,2,32]{3,5,4,2,1,0:T(8,128)S(1)} fusion(f32[4,2,32,32,32,1]{4,3,5,2,1,0:T(8,128)S(1)} %fusion, f32[4,2,32,32,32,1]{4,3,5,2,1,0:T(8,128)S(1)} %copy-done.1, f32[4]{0:T(128)S(1)} %get-tuple-element.30, f32[4]{0:T(128)S(1)} %get-tuple-element.29, f32[4]{0:T(128)S(1)} %get-tuple-element.11, f32[32,1,32]{2,0,1:T(8,128)S(1)} %get-tuple-element.33, ...), kind=kOutput, calls=%fused_computation.15 | convolution fusion | flops 204474368 | bytes 4202544 | tf_op jit(solution)/shard_map/...uw,wdq->...udq/dot_general | solution.py:54
  252.5 8.9 %fusion.26 = f32[4,2,32,2,32,32]{4,5,3,2,1,0:T(8,128)} fusion(f32[4,2,32,32,2,32]{3,5,4,2,1,0:T(8,128)S(1)} %fusion.13, f32[1,32,2,32]{3,1,2,0:T(8,128)S(1)} %get-tuple-element.28, f32[1,32,2,32]{3,1,2,0:T(8,128)S(1)} %get-tuple-element.27), kind=kOutput, calls=%fused_computation.29 | convolution fusion | flops 402657280 | bytes 4210688 | tf_op jit(solution)/shard_map/cpdu,...udq->...cpq/dot_general | solution.py:61
  261.5 8.9 %copy.83 = f32[4,2,32,2,32,32]{5,4,3,2,1,0:T(8,128)} copy(f32[4,2,32,2,32,32]{4,5,3,2,1,0:T(8,128)} %fusion.26) | data formatting | bytes 4194304 | tf_op jit(solution)/shard_map/cpdu,...udq->...cpq/transpose | solution.py:61
  270.4 7.7 %reshape.508 = f32[4,2,32,2048]{3,2,1,0:T(8,128)} reshape(f32[4,2,32,2,32,32]{5,4,3,2,1,0:T(8,128)} %copy.83) | data formatting | bytes 4194304 | tf_op jit(solution)/shard_map/reshape | solution.py:68
  278.1 2.3 subtract_reduce_fusion
  280.4 0.4 multiply_add_fusion.2
  280.9 0.2 pad_maximum_fusion.2
  281.1 2.7 fusion.72
  283.8 4.4 copy.87
  288.2 4.9 all-to-all-start
  293.2 0.1 reshape.548
  293.3 48.2 %all-to-all-done = f32[8,2,32,2048]{3,2,1,0:T(8,128)} async-done(((f32[8,2,32,2048]{3,2,1,0:T(8,128)}), f32[8,2,32,2048]{3,2,1,0:T(8,128)}, u32[]{:S(2)}, u32[]{:S(2)}) %all-to-all-start) | async-done | bytes 4194336 | tf_op jit(solution)/shard_map/all_to_all | solution.py:166
  341.5 3.1 reduce_sum.119
  344.6 0.5 convolution_bitcast_fusion
  345.1 0.3 fusion.39
  345.5 0.7 div.88
  346.2 142.3 %all-reduce.2.cloned.1.call-done = f32[1,32,2048]{2,1,0:T(8,128)} async-done(((f32[1,32,2048]{2,1,0:T(8,128)}), f32[1,32,2048]{2,1,0:T(8,128)}) %all-reduce.2.cloned.1.call-update) | async-done | bytes 262160 | tf_op jit(solution)/shard_map/psum | solution.py:168
  488.5 0.9 dynamic-slice_reduce_fusion
  489.5 0.3 convolution_bitcast_fusion.4
  489.8 0.8 multiply_reduce_fusion
  491.3 0.1 div.96
  491.4 0.6 multiply_reduce_fusion.1
  492.7 0.6 broadcast_divide_fusion
  (31 shorter events, 0.6 us)
Async XLA Ops:
  7.2 112.6 %all-gather.2.cloned.1.call-start = ((), (), s32[]{:S(2)}) async-start(), calls=%async_computation.1 | async-start | bytes 2105344 | tf_op jit(solution)/shard_map/all_gather | solution.py:136
  171.2 7.2 %copy-start = (f32[4,2,32,32,32,1]{4,3,5,2,1,0:T(8,128)}, f32[4,2,32,32,32,1]{4,3,5,2,1,0:T(8,128)S(1)}, u32[]{:S(2)}) copy-start(f32[4,2,32,32,32,1]{4,3,5,2,1,0:T(8,128)S(1)} %fusion.4) | copy-start | bytes 3145732
  237.0 6.7 %copy-start.1 = (f32[4,2,32,32,32,1]{4,3,5,2,1,0:T(8,128)S(1)}, f32[4,2,32,32,32,1]{4,3,5,2,1,0:T(8,128)}, u32[]{:S(2)}) copy-start(f32[4,2,32,32,32,1]{4,3,5,2,1,0:T(8,128)} %copy-done) | copy-start | bytes 3145732
  278.1 2.3 copy-start.2
  288.2 53.3 %all-to-all-start = ((f32[8,2,32,2048]{3,2,1,0:T(8,128)}), f32[8,2,32,2048]{3,2,1,0:T(8,128)}, u32[]{:S(2)}, u32[]{:S(2)}) async-start(f32[8,2,32,2048]{3,2,1,0:T(8,128)} %copy.87), calls=%async_computation | async-start | bytes 8388608 | tf_op jit(solution)/shard_map/all_to_all | solution.py:166
  293.2 195.3 %all-reduce.2.cloned.1.call-start = ((), (), s32[]{:S(2)}) async-start(), calls=%async_computation.2 | async-start | bytes 524288 | tf_op jit(solution)/shard_map/psum | solution.py:168
Sparse Core Ops, SparseCore 0:
  12.8 106.9 all-gather.1
  344.8 143.7 all-reduce.1
where the time goes:
time: 506 us; the launch traced here: 501 us
  waiting for transfers between devices  295 us (58%)
  matrix products  104 us (21%)
  local copies, waits for them, and re-layouts  61.4 us (12%)
  other arithmetic  18.9 us (4%)
  between operations  16.9 us (3%)
    psum x1, waiting for transfers between devices, on_device(): total = lax.psum(owner_sum, 'tile')  142 us
    all_gather x1, waiting for transfers between devices, on_device(): every = lax.all_gather(own_spec, ('tile', 'atom'), axis=0, tiled=True)  104 us
    all_to_all x1, waiting for transfers between devices, on_device(): lax.all_to_all(outgoing, 'atom', split_axis=0, concat_axis=1, tiled=True)  48.2 us
    dot_general x4, matrix products, inverse(): jnp.einsum('...cpq,cqew->...pew', shaped, inverse_right, precision=highes...  47.3 us
    dot_general x4, matrix products, inverse(): jnp.einsum('lmq,...qlg->...mg', inverse_left, across, precision=highest,...  18.6 us
    dot_general x4, matrix products, forward(): jnp.einsum('cpdu,...udq->...cpq', forward_left, across, precision=highest...  18.4 us
    transpose x4, local copies, waits for them, and re-layouts, forward(): jnp.einsum('cpdu,...udq->...cpq', forward_left, across, precision=highest...  18 us
    dot_general x4, matrix products, forward(): jnp.einsum('...uw,wdq->...udq', field, forward_right, precision=highest,...  16.8 us
  transfers between devices with their start and end apart: 3, of which 3 were waited for; matrix products, arithmetic and copies ran while one was open for 1% of the time, Pallas kernels for 0%

commit v1 on v0

--- a/solution.py
+++ b/solution.py
@@ -14,6 +14,17 @@
 step_ratio = 0.5
 epsilon = 1e-06
 highest = lax.Precision.HIGHEST
+
+
+def _raise_views(view, in_dim):
+    newest = lax.all_to_all(
+        jnp.stack(tuple((view for _ in range(lax.axis_size(("tile", "atom"))))), axis=0),
+        axis_name=("tile", "atom"),
+        split_axis=0,
+        concat_axis=0,
+    )
+    all_values = jnp.concatenate(newest, axis=in_dim)
+    return all_values
 
 
 def momentum_weights(count):
@@ -133,7 +144,7 @@
     code_spec = jnp.zeros((tiles_here, ACT, BLK, 2 * pixels), jnp.float32)
     weights = momentum_weights(ITERS)
     own_spec = forward(atoms, table)
-    every = lax.all_gather(own_spec, ("tile", "atom"), axis=0, tiled=True)
+    every = _raise_views(own_spec, 0)
     tile_groups = lax.axis_size("tile")
     every = every.reshape(tile_groups, NBLK, rows_owned, 2 * pixels)
     chosen = jnp.take(every, flat_ids, axis=1)

time: 506 us -> 468 us (0.925)
  waiting for transfers between devices: 295 us -> 240 us
  starting transfers between devices: 4.99 us -> 19.5 us
    all_gather x1 -> x0, waiting for transfers between devices: 104 us -> none  [on_device(): every = lax.all_gather(own_spec, ('tile', 'atom'), axis=0, tiled=True)]
    all_to_all x0 -> x1, waiting for transfers between devices: none -> 51.9 us  [_raise_views(): lax.all_to_all(jnp.stack(tuple((view for _ in range(lax.axis_size(('tile'...]
    all_to_all x0 -> x1, starting transfers between devices: none -> 14.6 us  [_raise_views(): lax.all_to_all(jnp.stack(tuple((view for _ in range(lax.axis_size(('tile'...]
    reshape x4 -> x3, local copies, waits for them, and re-layouts: 16.2 us -> 15.3 us  [forward(): return result.reshape(values.shape[:-1] + (2 * length * length,))]
where the time goes in v1:
time: 468 us; the launch traced here: 459 us
  waiting for transfers between devices  240 us (51%)
  matrix products  104 us (22%)
  local copies, waits for them, and re-layouts  59.8 us (13%)
  starting transfers between devices  19.5 us (4%)
  other arithmetic  18.9 us (4%)
  between operations  16.9 us (4%)
    psum x1, waiting for transfers between devices, on_device(): total = lax.psum(owner_sum, 'tile')  139 us
    all_to_all x1, waiting for transfers between devices, _raise_views(): lax.all_to_all(jnp.stack(tuple((view for _ in range(lax.axis_size(('tile'...  51.9 us
    all_to_all x1, waiting for transfers between devices, on_device(): lax.all_to_all(outgoing, 'atom', split_axis=0, concat_axis=1, tiled=True)  48.2 us
    dot_general x4, matrix products, inverse(): jnp.einsum('...cpq,cqew->...pew', shaped, inverse_right, precision=highes...  47.5 us
    dot_general x4, matrix products, forward(): jnp.einsum('cpdu,...udq->...cpq', forward_left, across, precision=highest...  18.8 us
    dot_general x4, matrix products, inverse(): jnp.einsum('lmq,...qlg->...mg', inverse_left, across, precision=highest,...  18.4 us
    transpose x4, local copies, waits for them, and re-layouts, forward(): jnp.einsum('cpdu,...udq->...cpq', forward_left, across, precision=highest...  18 us
    dot_general x4, matrix products, forward(): jnp.einsum('...uw,wdq->...udq', field, forward_right, precision=highest,...  16.8 us
  transfers between devices with their start and end apart: 3, of which 3 were waited for; matrix products, arithmetic and copies ran while one was open for 1% of the time, Pallas kernels for 0%

profile of v1, /device:TPU:8, one launch (start us, length us, event | category | flops | bytes accessed | tf_op | source)
XLA Modules:
  0.0 458.9 jit_solution(4038994808032598931)
XLA Ops:
  7.2 0.1 fusion.71
  7.3 0.1 fusion.70
  7.4 1.3 multiply_reduce_fusion.2
  9.4 0.5 broadcast.417
  9.9 1.3 fusion.91
  11.3 0.2 convolution_bitcast_fusion.6
  11.6 0.3 convolution_bitcast_fusion.5
  12.0 2.4 stack.22
  14.4 14.6 %all-to-all-start = ((f32[256,1,1,2048]{3,2,1,0:T(1,128)}), f32[256,1,1,2048]{3,2,1,0:T(1,128)S(1)}, u32[]{:S(2)}, u32[]{:S(2)}) async-start(f32[256,1,1,2048]{3,2,1,0:T(1,128)} %stack.22), calls=%async_computation | async-start | bytes 4194304 | tf_op jit(solution)/shard_map/all_to_all | solution.py:20
  29.0 0.1 copy.66
  29.1 0.1 reshape.497
  29.3 0.1 reshape.523
  29.4 0.5 convolution_bitcast_fusion.2
  29.9 0.3 convolution_bitcast_fusion.1
  30.2 0.1 copy.72
  30.3 0.1 reshape.500
  30.4 0.1 sine_negate_fusion
  30.5 0.2 convert_reduce_fusion
  30.8 51.9 %all-to-all-done = f32[256,1,1,2048]{3,2,1,0:T(1,128)S(1)} async-done(((f32[256,1,1,2048]{3,2,1,0:T(1,128)}), f32[256,1,1,2048]{3,2,1,0:T(1,128)S(1)}, u32[]{:S(2)}, u32[]{:S(2)}) %all-to-all-start) | async-done | bytes 2097184 | tf_op jit(solution)/shard_map/all_to_all | solution.py:20
  82.7 0.9 copy.160
  83.6 1.2 copy.70
  84.8 2.0 gather_fusion
  86.8 1.9 bitcast_select_fusion
  88.7 0.4 add_reduce_fusion.2
  89.2 0.3 multiply_add_fusion.4
  89.5 1.5 pad_maximum_fusion
  91.0 6.3 %reshape.527 = f32[4,2,32,2,32,32,1]{5,4,3,2,1,0,6:T(8,128)} reshape(f32[4,2,32,2048]{3,2,1,0:T(8,128)} %pad_maximum_fusion) | data formatting | bytes 4194304 | tf_op jit(solution)/shard_map/reshape | solution.py:85
  97.3 23.9 %fusion.6 = f32[4,2,32,32,2,32,1]{3,5,4,6,2,1,0:T(8,128)} fusion(f32[4,2,32,2,32,32,1]{5,4,3,2,1,0,6:T(8,128)} %reshape.527, f32[1,32,2,32]{3,1,2,0:T(8,128)S(1)} %get-tuple-element.28, f32[1,32,2,32]{3,1,2,0:T(8,128)S(1)} %get-tuple-element.27), kind=kOutput, calls=%fused_computation.7 | convolution fusion | flops 402657280 | bytes 4210688 | tf_op jit(solution)/shard_map/...cpq,cqew->...pew/dot_general | solution.py:86
  121.2 0.1 reduce_max.9
  121.3 10.7 %fusion.4 = f32[4,2,32,32,32,1]{4,3,5,2,1,0:T(8,128)S(1)} fusion(f32[4,2,32,32,2,32,1]{3,5,4,6,2,1,0:T(8,128)} %fusion.6, f32[1,32,32]{2,1,0:T(8,128)S(1)} %get-tuple-element.35, f32[1,32,32]{2,1,0:T(8,128)S(1)} %get-tuple-element.36), kind=kOutput, calls=%fused_computation.5 | convolution fusion | flops 201328640 | bytes 3153920 | tf_op jit(solution)/shard_map/lmq,...qlg->...mg/dot_general | solution.py:93
  132.1 7.1 %fusion.15 = f32[4,2,32,32,2,32]{3,5,4,2,1,0:T(8,128)S(1)} fusion(f32[4,2,32,32,32,1]{4,3,5,2,1,0:T(8,128)S(1)} %fusion.4, f32[4]{0:T(128)S(1)} %get-tuple-element.30, f32[4]{0:T(128)S(1)} %get-tuple-element.29, f32[4]{0:T(128)S(1)} %get-tuple-element.11, f32[32,1,32]{2,0,1:T(8,128)S(1)} %get-tuple-element.33, f32[32,1,32]{2,0,1:T(8,128)S(1)} %get-tuple-element.34), kind=kOutput, calls=%fused_computation.17 | convolution fusion | flops 202639360 | bytes 3153968 | tf_op jit(solution)/shard_map/...uw,wdq->...udq/dot_general | solution.py:65
  139.2 9.3 %fusion.23 = f32[4,2,32,2,32,32]{4,5,3,2,1,0:T(8,128)} fusion(f32[4,2,32,32,2,32]{3,5,4,2,1,0:T(8,128)S(1)} %fusion.15, f32[1,32,2,32]{3,1,2,0:T(8,128)S(1)} %get-tuple-element.28, f32[1,32,2,32]{3,1,2,0:T(8,128)S(1)} %get-tuple-element.27), kind=kOutput, calls=%fused_computation.28 | convolution fusion | flops 402657280 | bytes 4210688 | tf_op jit(solution)/shard_map/cpdu,...udq->...cpq/dot_general | solution.py:72
  148.5 8.9 %copy.78 = f32[4,2,32,2,32,32]{5,4,3,2,1,0:T(8,128)} copy(f32[4,2,32,2,32,32]{4,5,3,2,1,0:T(8,128)} %fusion.23) | data formatting | bytes 4194304 | tf_op jit(solution)/shard_map/cpdu,...udq->...cpq/transpose | solution.py:72
  157.5 7.5 %reshape.502 = f32[4,2,32,2048]{3,2,1,0:T(8,128)} reshape(f32[4,2,32,2,32,32]{5,4,3,2,1,0:T(8,128)} %copy.78) | data formatting | bytes 4194304 | tf_op jit(solution)/shard_map/reshape | solution.py:79
  165.0 1.8 multiply_add_fusion.1
  166.7 0.6 subtract_reduce_fusion.1
  167.3 0.3 multiply_add_fusion.3
  167.6 1.5 pad_maximum_fusion.1
  169.2 6.3 %reshape.537 = f32[4,2,32,2,32,32,1]{5,4,3,2,1,0,6:T(8,128)} reshape(f32[4,2,32,2048]{3,2,1,0:T(8,128)} %pad_maximum_fusion.1) | data formatting | bytes 4194304 | tf_op jit(solution)/shard_map/reshape | solution.py:85
  175.4 22.8 %fusion.2 = f32[4,2,32,32,2,32,1]{3,5,4,6,2,1,0:T(8,128)S(1)} fusion(f32[4,2,32,2,32,32,1]{5,4,3,2,1,0,6:T(8,128)} %reshape.537, f32[1,32,2,32]{3,1,2,0:T(8,128)S(1)} %get-tuple-element.28, f32[1,32,2,32]{3,1,2,0:T(8,128)S(1)} %get-tuple-element.27), kind=kOutput, calls=%fused_computation.3 | convolution fusion | flops 402657280 | bytes 4210688 | tf_op jit(solution)/shard_map/...cpq,cqew->...pew/dot_general | solution.py:86
  198.2 6.6 %fusion = f32[4,2,32,32,32,1]{4,3,5,2,1,0:T(8,128)S(1)} fusion(f32[4,2,32,32,2,32,1]{3,5,4,6,2,1,0:T(8,128)S(1)} %fusion.2, f32[1,32,32]{2,1,0:T(8,128)S(1)} %get-tuple-element.35, f32[1,32,32]{2,1,0:T(8,128)S(1)} %get-tuple-element.36), kind=kOutput, calls=%fused_computation.1 | convolution fusion | flops 201328640 | bytes 3153920 | tf_op jit(solution)/shard_map/lmq,...qlg->...mg/dot_general | solution.py:93
  204.9 8.9 %fusion.13 = f32[4,2,32,32,2,32]{3,5,4,2,1,0:T(8,128)S(1)} fusion(f32[4,2,32,32,32,1]{4,3,5,2,1,0:T(8,128)S(1)} %fusion, f32[4,2,32,32,32,1]{4,3,5,2,1,0:T(8,128)S(1)} %copy-done.1, f32[4]{0:T(128)S(1)} %get-tuple-element.30, f32[4]{0:T(128)S(1)} %get-tuple-element.29, f32[4]{0:T(128)S(1)} %get-tuple-element.11, f32[32,1,32]{2,0,1:T(8,128)S(1)} %get-tuple-element.33, ...), kind=kOutput, calls=%fused_computation.15 | convolution fusion | flops 204474368 | bytes 4202544 | tf_op jit(solution)/shard_map/...uw,wdq->...udq/dot_general | solution.py:65
  213.8 8.9 %fusion.26 = f32[4,2,32,2,32,32]{4,5,3,2,1,0:T(8,128)} fusion(f32[4,2,32,32,2,32]{3,5,4,2,1,0:T(8,128)S(1)} %fusion.13, f32[1,32,2,32]{3,1,2,0:T(8,128)S(1)} %get-tuple-element.28, f32[1,32,2,32]{3,1,2,0:T(8,128)S(1)} %get-tuple-element.27), kind=kOutput, calls=%fused_computation.29 | convolution fusion | flops 402657280 | bytes 4210688 | tf_op jit(solution)/shard_map/cpdu,...udq->...cpq/dot_general | solution.py:72
  222.7 8.9 %copy.83 = f32[4,2,32,2,32,32]{5,4,3,2,1,0:T(8,128)} copy(f32[4,2,32,2,32,32]{4,5,3,2,1,0:T(8,128)} %fusion.26) | data formatting | bytes 4194304 | tf_op jit(solution)/shard_map/cpdu,...udq->...cpq/transpose | solution.py:72
  231.7 7.7 %reshape.504 = f32[4,2,32,2048]{3,2,1,0:T(8,128)} reshape(f32[4,2,32,2,32,32]{5,4,3,2,1,0:T(8,128)} %copy.83) | data formatting | bytes 4194304 | tf_op jit(solution)/shard_map/reshape | solution.py:79
  239.4 2.3 subtract_reduce_fusion
  241.7 0.4 multiply_add_fusion.2
  242.1 0.2 pad_maximum_fusion.2
  242.4 2.7 fusion.72
  245.1 4.4 copy.87
  249.5 4.9 %all-to-all-start.1 = ((f32[8,2,32,2048]{3,2,1,0:T(8,128)}), f32[8,2,32,2048]{3,2,1,0:T(8,128)}, u32[]{:S(2)}, u32[]{:S(2)}) async-start(f32[8,2,32,2048]{3,2,1,0:T(8,128)} %copy.87), calls=%async_computation.1 | async-start | bytes 8388608 | tf_op jit(solution)/shard_map/all_to_all | solution.py:177
  254.5 0.1 reshape.544
  254.6 48.2 %all-to-all-done.1 = f32[8,2,32,2048]{3,2,1,0:T(8,128)} async-done(((f32[8,2,32,2048]{3,2,1,0:T(8,128)}), f32[8,2,32,2048]{3,2,1,0:T(8,128)}, u32[]{:S(2)}, u32[]{:S(2)}) %all-to-all-start.1) | async-done | bytes 4194336 | tf_op jit(solution)/shard_map/all_to_all | solution.py:177
  302.8 3.1 reduce_sum.119
  305.9 0.5 convolution_bitcast_fusion
  306.4 0.3 fusion.39
  306.7 0.7 div.88
  307.4 139.5 %all-reduce.2.cloned.1.call-done = f32[1,32,2048]{2,1,0:T(8,128)} async-done(((f32[1,32,2048]{2,1,0:T(8,128)}), f32[1,32,2048]{2,1,0:T(8,128)}) %all-reduce.2.cloned.1.call-update) | async-done | bytes 262160 | tf_op jit(solution)/shard_map/psum | solution.py:179
  446.9 0.9 dynamic-slice_reduce_fusion
  447.8 0.3 convolution_bitcast_fusion.4
  448.1 0.8 multiply_reduce_fusion
  449.7 0.1 div.96
  449.7 0.6 multiply_reduce_fusion.1
  451.1 0.6 broadcast_divide_fusion
  (35 shorter events, 0.7 us)
Async XLA Ops:
  7.2 21.9 %copy-start.4 = (s32[4,2]{0,1:T(2,128)S(1)}, s32[4,2]{0,1:T(2,128)}, u32[]{:S(2)}) copy-start(s32[4,2]{0,1:T(2,128)} %param.4) | copy-start | bytes 100
  7.2 22.1 %copy-start.3 = (f32[4,1024]{1,0:T(4,128)S(1)}, f32[4,1024]{1,0:T(4,128)}, u32[]{:S(2)}) copy-start(f32[4,1024]{1,0:T(4,128)} %param.3) | copy-start | bytes 49156
  14.4 68.3 %all-to-all-start = ((f32[256,1,1,2048]{3,2,1,0:T(1,128)}), f32[256,1,1,2048]{3,2,1,0:T(1,128)S(1)}, u32[]{:S(2)}, u32[]{:S(2)}) async-start(f32[256,1,1,2048]{3,2,1,0:T(1,128)} %stack.22), calls=%async_computation | async-start | bytes 4194304 | tf_op jit(solution)/shard_map/all_to_all | solution.py:20
  132.0 7.2 %copy-start = (f32[4,2,32,32,32,1]{4,3,5,2,1,0:T(8,128)}, f32[4,2,32,32,32,1]{4,3,5,2,1,0:T(8,128)S(1)}, u32[]{:S(2)}) copy-start(f32[4,2,32,32,32,1]{4,3,5,2,1,0:T(8,128)S(1)} %fusion.4) | copy-start | bytes 3145732
  198.2 6.7 %copy-start.1 = (f32[4,2,32,32,32,1]{4,3,5,2,1,0:T(8,128)S(1)}, f32[4,2,32,32,32,1]{4,3,5,2,1,0:T(8,128)}, u32[]{:S(2)}) copy-start(f32[4,2,32,32,32,1]{4,3,5,2,1,0:T(8,128)} %copy-done) | copy-start | bytes 3145732
  239.4 2.3 copy-start.2
  249.5 53.2 %all-to-all-start.1 = ((f32[8,2,32,2048]{3,2,1,0:T(8,128)}), f32[8,2,32,2048]{3,2,1,0:T(8,128)}, u32[]{:S(2)}, u32[]{:S(2)}) async-start(f32[8,2,32,2048]{3,2,1,0:T(8,128)} %copy.87), calls=%async_computation.1 | async-start | bytes 8388608 | tf_op jit(solution)/shard_map/all_to_all | solution.py:177
  254.4 192.4 %all-reduce.2.cloned.1.call-start = ((), (), s32[]{:S(2)}) async-start(), calls=%async_computation.2 | async-start | bytes 524288 | tf_op jit(solution)/shard_map/psum | solution.py:179
Sparse Core Ops, SparseCore 0:
  306.0 140.8 all-reduce.1
